TPU v7x, 128 devices: a whole 4x4x4 slice. The times are simulated.
128 devices in a mesh: dp: 16 (over x, z), fsdp: 8 (over y, core).
Axes of the slice: x: 4, y: 4, z: 4, core: 2. Of those that a mesh axis runs over, the one named last changes fastest.
Arguments:
- tokens: bfloat16 [2048, 4096], P('dp', 'fsdp'), may hold values from -6 to 6
- expert_ids: int32 [2048, 2], P('dp'), may hold values from 0 to 7, all different within a row; in each aligned block of 128 rows (0 to 127, 128 to 255, ...) at most 40 rows name the same one
- route_probs: float32 [2048, 2], P('dp'), may hold values from 0.1 to 0.9
- w_gate: bfloat16 [4096, 65536], P(None, ('dp', 'fsdp')), may hold values from -0.09375 to 0.09375
- w_up: bfloat16 [4096, 65536], P(None, ('dp', 'fsdp')), may hold values from -0.09375 to 0.09375
- w_down: bfloat16 [65536, 4096], P(('dp', 'fsdp')), may hold values from -0.0625 to 0.0625
- out_grad: bfloat16 [2048, 4096], P('dp', 'fsdp'), may hold values from -0.59765625 to 0.59765625
Outputs:
- mixed: bfloat16 [2048, 4096], P('dp', 'fsdp')
- token_grad: bfloat16 [2048, 4096], P('dp', 'fsdp')
- prob_grad: float32 [2048, 2], P('dp')
- gate_weight_grad: bfloat16 [4096, 65536], P(None, ('dp', 'fsdp'))
- up_weight_grad: bfloat16 [4096, 65536], P(None, ('dp', 'fsdp'))
- down_weight_grad: bfloat16 [65536, 4096], P(('dp', 'fsdp'))
Inputs may be any that keep to these rules, and one draw needn't show every extreme that they name: `expert_ids`: each token names two different experts. Within the 128 tokens of one dp index (aligned blocks of rows) no expert is named more than 40 times, and in some block one expert is named exactly 40 times.
All inputs are finite; a program needn't handle non-finite values.
Results may differ from a plain program's by a relative error of at most 0.019.
Values may be sent and summed in bfloat16 or wider, within the bound.
No kernel may reach another device: no remote copies, remote signals or barrier semaphores. Data moves between devices by JAX's collectives and lax.ppermute only.
A program may use at most 128 MiB of HBM per device.

v0:
```python
import jax
import jax.numpy as jnp
from jax import lax
from jax.sharding import PartitionSpec as P

E = 8
CAP = 40


def local(tokens, expert_ids, route_probs, w_gate, w_up, w_down, out_grad):
    dp_count = lax.axis_size("dp")
    groups = dp_count // E
    token_count = tokens.shape[0]
    slot_total = E * CAP
    routing = expert_ids.reshape(-1)
    onehot = (routing[:, None] == jnp.arange(E, dtype=jnp.int32)[None, :]).astype(jnp.int32)
    position = jnp.sum((jnp.cumsum(onehot, axis=0) - onehot) * onehot, axis=1)
    slot_of = (routing * CAP + position).reshape(token_count, 2)
    slot_index = jnp.arange(slot_total, dtype=jnp.int32)
    select_first = slot_of[:, 0:1] == slot_index[None, :]
    select_second = slot_of[:, 1:2] == slot_index[None, :]
    picker = jnp.logical_or(select_first, select_second)
    picker_bf = picker.astype(jnp.bfloat16)
    weighted = jnp.where(select_first, route_probs[:, 0:1], 0.0) + jnp.where(
        select_second, route_probs[:, 1:2], 0.0
    )
    contract_rows = (((0,), (0,)), ((), ()))
    back_dims = (((1,), (1,)), ((), ()))

    def place_rows(source, scaled):
        if scaled:
            placed = lax.dot_general(
                weighted,
                source.astype(jnp.float32),
                contract_rows,
                precision=lax.Precision.HIGHEST,
                preferred_element_type=jnp.float32,
            )
        else:
            placed = lax.dot_general(
                picker_bf, source, contract_rows, preferred_element_type=jnp.float32
            )
        placed = placed.astype(jnp.bfloat16).reshape(E, CAP, source.shape[1])
        return jnp.repeat(placed, groups, axis=0)

    def to_expert_layout(source, scaled):
        joined = lax.all_gather(source, "fsdp", axis=1, tiled=True)
        arrived = lax.all_to_all(
            place_rows(joined, scaled), "dp", split_axis=0, concat_axis=0, tiled=True
        )
        return arrived.reshape(dp_count * CAP, arrived.shape[2])

    def to_token_layout(partial_value):
        shares = lax.psum_scatter(
            partial_value.astype(jnp.bfloat16), "fsdp", scatter_dimension=1, tiled=True
        ).astype(jnp.float32)
        returned = lax.all_to_all(
            shares.reshape(dp_count, CAP, shares.shape[1]).astype(jnp.bfloat16),
            "dp",
            split_axis=0,
            concat_axis=0,
            tiled=True,
        ).astype(jnp.float32)
        return jnp.sum(returned.reshape(E, groups, CAP, returned.shape[2]), axis=1).reshape(
            slot_total, returned.shape[2]
        )

    expert_rows = to_expert_layout(tokens, False)
    gate_proj = jnp.dot(expert_rows, w_gate, preferred_element_type=jnp.float32)
    up_proj = jnp.dot(expert_rows, w_up, preferred_element_type=jnp.float32)
    sigmoid_gate = jax.nn.sigmoid(gate_proj)
    activated = gate_proj * sigmoid_gate
    hidden = (activated * up_proj).astype(jnp.bfloat16)
    out_partial = jnp.dot(hidden, w_down, preferred_element_type=jnp.float32)
    out_slots = to_token_layout(out_partial)
    first_pair = jnp.dot(
        select_first.astype(jnp.float32),
        out_slots,
        precision=lax.Precision.HIGHEST,
        preferred_element_type=jnp.float32,
    )
    second_pair = jnp.dot(
        select_second.astype(jnp.float32),
        out_slots,
        precision=lax.Precision.HIGHEST,
        preferred_element_type=jnp.float32,
    )
    mixed = (route_probs[:, 0:1] * first_pair + route_probs[:, 1:2] * second_pair).astype(
        jnp.bfloat16
    )
    grad_local = out_grad.astype(jnp.float32)
    prob_terms = jnp.stack(
        [jnp.sum(first_pair * grad_local, axis=1), jnp.sum(second_pair * grad_local, axis=1)],
        axis=1,
    )
    prob_grad = lax.psum(prob_terms, "fsdp")
    grad_rows = to_expert_layout(out_grad, True)
    hidden_grad = lax.dot_general(grad_rows, w_down, back_dims, preferred_element_type=jnp.float32)
    gate_grad = (
        hidden_grad * up_proj * sigmoid_gate * (1.0 + gate_proj * (1.0 - sigmoid_gate))
    ).astype(jnp.bfloat16)
    up_grad = (hidden_grad * activated).astype(jnp.bfloat16)
    gate_weight_grad = lax.dot_general(
        expert_rows, gate_grad, contract_rows, preferred_element_type=jnp.float32
    ).astype(jnp.bfloat16)
    up_weight_grad = lax.dot_general(
        expert_rows, up_grad, contract_rows, preferred_element_type=jnp.float32
    ).astype(jnp.bfloat16)
    down_weight_grad = lax.dot_general(
        hidden, grad_rows, contract_rows, preferred_element_type=jnp.float32
    ).astype(jnp.bfloat16)
    input_partial = lax.dot_general(
        gate_grad, w_gate, back_dims, preferred_element_type=jnp.float32
    )
    input_partial = input_partial + lax.dot_general(
        up_grad, w_up, back_dims, preferred_element_type=jnp.float32
    )
    input_slots = to_token_layout(input_partial)
    token_grad = jnp.dot(
        picker.astype(jnp.float32),
        input_slots,
        precision=lax.Precision.HIGHEST,
        preferred_element_type=jnp.float32,
    ).astype(jnp.bfloat16)
    return (mixed, token_grad, prob_grad, gate_weight_grad, up_weight_grad, down_weight_grad)


def solution(mesh):
    placed = (
        P("dp", "fsdp"),
        P("dp", None),
        P("dp", None),
        P(None, ("dp", "fsdp")),
        P(None, ("dp", "fsdp")),
        P(("dp", "fsdp"), None),
        P("dp", "fsdp"),
    )
    return jax.shard_map(
        local,
        mesh=mesh,
        in_specs=placed,
        out_specs=(
            P("dp", "fsdp"),
            P("dp", "fsdp"),
            P("dp", None),
            P(None, ("dp", "fsdp")),
            P(None, ("dp", "fsdp")),
            P(("dp", "fsdp"), None),
        ),
        check_vma=False,
    )
```

profile of v0, /device:TPU:2, one launch (start us, length us, event | category | flops | bytes accessed | tf_op | source)
XLA Modules:
  0.0 347.4 jit_solution(6366988755404527250)
XLA Ops:
  10.8 24.6 %all-gather.3.cloned.1.call-done = bf16[128,4096]{1,0:T(8,128)(2,1)} async-done(((bf16[128,512]{1,0:T(8,128)(2,1)}), bf16[128,4096]{1,0:T(8,128)(2,1)}) %all-gather.3.cloned.1.call-update) | async-done | bytes 1048592 | tf_op jit(solution)/shard_map/all_gather | solution.py:47
  35.5 2.2 convolution_convert_fusion.5
  37.6 3.0 broadcast_in_dim.27
  40.6 7.5 %all-to-all-start = ((bf16[16,40,4096]{2,1,0:T(8,128)(2,1)}), bf16[16,40,4096]{2,1,0:T(8,128)(2,1)}, u32[]{:S(2)}, u32[]{:S(2)}) async-start(bf16[16,40,4096]{2,1,0:T(8,128)(2,1)} %bitcast.57), calls=%async_computation | async-start | bytes 10485760 | tf_op jit(solution)/shard_map/all_to_all | solution.py:48
  49.0 24.8 %all-gather.5.cloned.1.call-done = bf16[128,4096]{1,0:T(8,128)(2,1)} async-done(((bf16[128,512]{1,0:T(8,128)(2,1)}), bf16[128,4096]{1,0:T(8,128)(2,1)}) %all-gather.5.cloned.1.call-update) | async-done | bytes 1048592 | tf_op jit(solution)/shard_map/all_gather | solution.py:47
  73.8 3.6 %convolution_convert_fusion.4 = bf16[320,4096]{1,0:T(8,128)(2,1)S(1)} fusion(bf16[128,4096]{1,0:T(8,128)(2,1)} %all-gather.5.cloned.1.call-done, f32[128]{0:T(128)S(1)} %get-tuple-element.13, f32[128]{0:T(128)S(1)} %get-tuple-element.12, s32[128]{0:T(128)S(1)} %get-tuple-element.15, s32[128]{0:T(128)S(1)} %get-tuple-element.14), kind=kOutput, calls=%fused_computation.5 | convolution fusion | flops 2014781440 | bytes 3672064 | tf_op jit(solution)/shard_map/dot_general | solution.py:32
  77.4 38.4 %all-to-all-done = bf16[16,40,4096]{2,1,0:T(8,128)(2,1)} async-done(((bf16[16,40,4096]{2,1,0:T(8,128)(2,1)}), bf16[16,40,4096]{2,1,0:T(8,128)(2,1)}, u32[]{:S(2)}, u32[]{:S(2)}) %all-to-all-start) | async-done | bytes 5242912 | tf_op jit(solution)/shard_map/all_to_all | solution.py:48
  115.7 3.0 broadcast_in_dim.31
  118.7 24.0 %all-to-all-start.2 = ((bf16[16,40,4096]{2,1,0:T(8,128)(2,1)}), bf16[16,40,4096]{2,1,0:T(8,128)(2,1)}, u32[]{:S(2)}, u32[]{:S(2)}) async-start(bf16[16,40,4096]{2,1,0:T(8,128)(2,1)} %bitcast.58), calls=%async_computation.3 | async-start | bytes 10485760 | tf_op jit(solution)/shard_map/all_to_all | solution.py:48
  143.0 7.8 %fusion.26 = f32[640,512]{1,0:T(8,128)} fusion(bf16[640,4096]{1,0:T(8,128)(2,1)} %bitcast.7, bf16[4096,512]{1,0:T(8,128)(2,1)} %param.10), kind=kOutput, calls=%fused_computation.53 | convolution fusion | flops 2684354560 | bytes 10747904 | tf_op jit(solution)/shard_map/dot_general | solution.py:69
  150.8 6.4 %fusion.27 = f32[640,512]{1,0:T(8,128)} fusion(bf16[640,4096]{1,0:T(8,128)(2,1)} %bitcast.7, bf16[4096,512]{1,0:T(8,128)(2,1)S(1)} %copy-done.3), kind=kOutput, calls=%fused_computation.54 | convolution fusion | flops 2684354560 | bytes 10747904 | tf_op jit(solution)/shard_map/dot_general | solution.py:70
  157.2 53.1 %all-to-all-done.2 = bf16[16,40,4096]{2,1,0:T(8,128)(2,1)} async-done(((bf16[16,40,4096]{2,1,0:T(8,128)(2,1)}), bf16[16,40,4096]{2,1,0:T(8,128)(2,1)}, u32[]{:S(2)}, u32[]{:S(2)}) %all-to-all-start.2) | async-done | bytes 5242912 | tf_op jit(solution)/shard_map/all_to_all | solution.py:48
  210.3 8.0 %multiply_convert_fusion = (bf16[640,512]{1,0:T(8,128)(2,1)S(1)}, bf16[640,512]{1,0:T(8,128)(2,1)S(1)}, bf16[640,512]{1,0:T(8,128)(2,1)S(1)}) fusion(f32[640,512]{1,0:T(8,128)} %fusion.26, f32[640,512]{1,0:T(8,128)} %fusion.27, bf16[640,4096]{1,0:T(8,128)(2,1)} %bitcast.14, bf16[512,4096]{1,0:T(8,128)(2,1)} %param.12), kind=kOutput, calls=%fused_computation.9 | convolution fusion | flops 2689269760 | bytes 14024704 | tf_op jit(solution)/shard_map/dot_general | solution.py:98
  218.3 4.7 %convolution_convert_fusion = bf16[640,4096]{1,0:T(8,128)(2,1)} fusion(bf16[640,512]{1,0:T(8,128)(2,1)S(1)} %get-tuple-element.10, bf16[512,4096]{1,0:T(8,128)(2,1)S(1)} %copy-done.2), kind=kOutput, calls=%fused_computation.1 | convolution fusion | flops 2686976000 | bytes 10092544 | tf_op jit(solution)/shard_map/dot_general | solution.py:74
  223.3 4.9 %fusion.28 = f32[640,4096]{1,0:T(8,128)S(1)} fusion(bf16[640,512]{1,0:T(8,128)(2,1)S(1)} %get-tuple-element.9, bf16[4096,512]{1,0:T(8,128)(2,1)} %param.10), kind=kOutput, calls=%fused_computation.55 | convolution fusion | flops 2684354560 | bytes 15335424 | tf_op jit(solution)/shard_map/dot_general | solution.py:112
  228.2 4.8 %add_convert_fusion = bf16[640,4096]{1,0:T(8,128)(2,1)} fusion(f32[640,4096]{1,0:T(8,128)S(1)} %fusion.28, bf16[640,512]{1,0:T(8,128)(2,1)S(1)} %get-tuple-element.8, bf16[4096,512]{1,0:T(8,128)(2,1)S(1)} %copy-done.4), kind=kOutput, calls=%fused_computation | convolution fusion | flops 2689597440 | bytes 20578304 | tf_op jit(solution)/shard_map/dot_general | solution.py:115
  233.0 7.5 %convolution_convert_fusion.1 = bf16[512,4096]{1,0:T(8,128)(2,1)} fusion(bf16[640,512]{1,0:T(8,128)(2,1)S(1)} %get-tuple-element.10, bf16[640,4096]{1,0:T(8,128)(2,1)} %bitcast.14), kind=kOutput, calls=%fused_computation.2 | convolution fusion | flops 2686451712 | bytes 10092544 | tf_op jit(solution)/shard_map/dot_general | solution.py:109
  240.5 7.5 %convolution_convert_fusion.2 = bf16[4096,512]{1,0:T(8,128)(2,1)} fusion(bf16[640,4096]{1,0:T(8,128)(2,1)} %bitcast.7, bf16[640,512]{1,0:T(8,128)(2,1)S(1)} %get-tuple-element.8), kind=kOutput, calls=%fused_computation.3 | convolution fusion | flops 2686451712 | bytes 10092544 | tf_op jit(solution)/shard_map/dot_general | solution.py:106
  248.0 26.8 %reduce-scatter.3.cloned.1.call-done = bf16[640,512]{1,0:T(8,128)(2,1)} async-done(((bf16[640,4096]{1,0:T(8,128)(2,1)}), bf16[640,512]{1,0:T(8,128)(2,1)}) %reduce-scatter.3.cloned.1.call-update) | async-done | bytes 655376 | tf_op jit(solution)/shard_map/reduce_scatter | solution.py:54
  274.8 7.5 %all-to-all-start.1 = ((bf16[16,40,512]{2,1,0:T(8,128)(2,1)}), bf16[16,40,512]{2,1,0:T(8,128)(2,1)S(1)}, u32[]{:S(2)}, u32[]{:S(2)}) async-start(bf16[16,40,512]{2,1,0:T(8,128)(2,1)} %bitcast.65), calls=%async_computation.2 | async-start | bytes 1310720 | tf_op jit(solution)/shard_map/all_to_all | solution.py:57
  282.3 7.6 %convolution_convert_fusion.3 = bf16[4096,512]{1,0:T(8,128)(2,1)} fusion(bf16[640,4096]{1,0:T(8,128)(2,1)} %bitcast.7, bf16[640,512]{1,0:T(8,128)(2,1)S(1)} %get-tuple-element.9), kind=kOutput, calls=%fused_computation.4 | convolution fusion | flops 2686451712 | bytes 10092544 | tf_op jit(solution)/shard_map/dot_general | solution.py:103
  289.9 26.6 %reduce-scatter.5.cloned.1.call-done = bf16[640,512]{1,0:T(8,128)(2,1)} async-done(((bf16[640,4096]{1,0:T(8,128)(2,1)}), bf16[640,512]{1,0:T(8,128)(2,1)}) %reduce-scatter.5.cloned.1.call-update) | async-done | bytes 655376 | tf_op jit(solution)/shard_map/reduce_scatter | solution.py:54
  316.5 7.5 %all-to-all-start.3 = ((bf16[16,40,512]{2,1,0:T(8,128)(2,1)}), bf16[16,40,512]{2,1,0:T(8,128)(2,1)S(1)}, u32[]{:S(2)}, u32[]{:S(2)}) async-start(bf16[16,40,512]{2,1,0:T(8,128)(2,1)} %bitcast.64), calls=%async_computation.5 | async-start | bytes 1310720 | tf_op jit(solution)/shard_map/all_to_all | solution.py:57
  325.7 13.9 %psum.7 = f32[128,2]{0,1:T(2,128)} all-reduce(f32[128,2]{0,1:T(2,128)S(1)} %pad_maximum_fusion), channel_id=1, replica_groups=mesh['dp'=16,'fsdp'=8] {'fsdp'}, use_global_device_ids=true, to_apply=%region_9.10 | all-reduce | flops 256 | bytes 2048 | tf_op jit(solution)/shard_map/psum | solution.py:96
  (40 shorter events, 7.8 us)
Async XLA Ops:
  7.2 28.3 %all-gather.3.cloned.1.call-start = ((), (), s32[]{:S(2)}) async-start(), calls=%async_computation.6 | async-start | bytes 1179648 | tf_op jit(solution)/shard_map/all_gather | solution.py:47
  40.6 8.3 %copy-start.1 = (f32[128,2]{0,1:T(2,128)S(1)}, f32[128,2]{0,1:T(2,128)}, u32[]{:S(2)}) copy-start(f32[128,2]{0,1:T(2,128)} %param.9) | copy-start | bytes 3076
  40.6 75.1 %all-to-all-start = ((bf16[16,40,4096]{2,1,0:T(8,128)(2,1)}), bf16[16,40,4096]{2,1,0:T(8,128)(2,1)}, u32[]{:S(2)}, u32[]{:S(2)}) async-start(bf16[16,40,4096]{2,1,0:T(8,128)(2,1)} %bitcast.57), calls=%async_computation | async-start | bytes 10485760 | tf_op jit(solution)/shard_map/all_to_all | solution.py:48
  48.2 25.6 %all-gather.5.cloned.1.call-start = ((), (), s32[]{:S(2)}) async-start(), calls=%async_computation.8 | async-start | bytes 1179648 | tf_op jit(solution)/shard_map/all_gather | solution.py:47
  118.7 91.6 %all-to-all-start.2 = ((bf16[16,40,4096]{2,1,0:T(8,128)(2,1)}), bf16[16,40,4096]{2,1,0:T(8,128)(2,1)}, u32[]{:S(2)}, u32[]{:S(2)}) async-start(bf16[16,40,4096]{2,1,0:T(8,128)(2,1)} %bitcast.58), calls=%async_computation.3 | async-start | bytes 10485760 | tf_op jit(solution)/shard_map/all_to_all | solution.py:48
  142.7 132.1 %reduce-scatter.3.cloned.1.call-start = ((), (), s32[]{:S(2)}) async-start(), calls=%async_computation.7 | async-start | bytes 5898240 | tf_op jit(solution)/shard_map/reduce_scatter | solution.py:54
  142.9 7.8 %copy-start.3 = (bf16[4096,512]{1,0:T(8,128)(2,1)S(1)}, bf16[4096,512]{1,0:T(8,128)(2,1)}, u32[]{:S(2)}) copy-start(bf16[4096,512]{1,0:T(8,128)(2,1)} %param.11) | copy-start | bytes 12582916
  210.3 8.0 %copy-start.2 = (bf16[512,4096]{1,0:T(8,128)(2,1)S(1)}, bf16[512,4096]{1,0:T(8,128)(2,1)}, u32[]{:S(2)}) copy-start(bf16[512,4096]{1,0:T(8,128)(2,1)} %param.12) | copy-start | bytes 12582916
  223.0 93.5 %reduce-scatter.5.cloned.1.call-start = ((), (), s32[]{:S(2)}) async-start(), calls=%async_computation.9 | async-start | bytes 5898240 | tf_op jit(solution)/shard_map/reduce_scatter | solution.py:54
  223.3 4.9 %copy-start.4 = (bf16[4096,512]{1,0:T(8,128)(2,1)S(1)}, bf16[4096,512]{1,0:T(8,128)(2,1)}, u32[]{:S(2)}) copy-start(bf16[4096,512]{1,0:T(8,128)(2,1)} %param.11) | copy-start | bytes 12582916
  274.8 41.7 %all-to-all-start.1 = ((bf16[16,40,512]{2,1,0:T(8,128)(2,1)}), bf16[16,40,512]{2,1,0:T(8,128)(2,1)S(1)}, u32[]{:S(2)}, u32[]{:S(2)}) async-start(bf16[16,40,512]{2,1,0:T(8,128)(2,1)} %bitcast.65), calls=%async_computation.2 | async-start | bytes 1310720 | tf_op jit(solution)/shard_map/all_to_all | solution.py:57
  282.2 42.3 %copy-start = (bf16[128,512]{1,0:T(8,128)(2,1)S(1)}, bf16[128,512]{1,0:T(8,128)(2,1)}, u32[]{:S(2)}) copy-start(bf16[128,512]{1,0:T(8,128)(2,1)} %param.13) | copy-start | bytes 393220
  316.5 23.1 %all-to-all-start.3 = ((bf16[16,40,512]{2,1,0:T(8,128)(2,1)}), bf16[16,40,512]{2,1,0:T(8,128)(2,1)S(1)}, u32[]{:S(2)}, u32[]{:S(2)}) async-start(bf16[16,40,512]{2,1,0:T(8,128)(2,1)} %bitcast.64), calls=%async_computation.5 | async-start | bytes 1310720 | tf_op jit(solution)/shard_map/all_to_all | solution.py:57
Sparse Core Ops, SparseCore 0:
  9.7 25.7 all-gather.2
  50.7 23.0 all-gather.4
  223.1 51.6 reduce-scatter.2
  277.0 39.3 reduce-scatter.4
where the time goes:
time: 348 us; the launch traced here: 347 us
  waiting for transfers between devices  196 us (56%)
  matrix products  67.6 us (19%)
  starting transfers between devices  47 us (14%)
  blocking collectives  13.9 us (4%)
  between operations  13.9 us (4%)
  local copies, waits for them, and re-layouts  7.52 us (2%)
    all_to_all x2, waiting for transfers between devices, to_expert_layout(): lax.all_to_all(place_rows(joined, scaled), 'dp', split_axis=0, concat_axi...  91.5 us
    reduce_scatter x2, waiting for transfers between devices, to_token_layout(): lax.psum_scatter(partial_value.astype(jnp.bfloat16), 'fsdp', scatter_dime...  53.4 us
    all_gather x2, waiting for transfers between devices, to_expert_layout(): joined = lax.all_gather(source, 'fsdp', axis=1, tiled=True)  49.5 us
    all_to_all x2, starting transfers between devices, to_expert_layout(): lax.all_to_all(place_rows(joined, scaled), 'dp', split_axis=0, concat_axi...  31.5 us
    all_to_all x2, starting transfers between devices, to_token_layout(): lax.all_to_all(shares.reshape(dp_count, CAP, shares.shape[1]).astype(jnp....  15 us
    psum x1, blocking collectives, local(): prob_grad = lax.psum(prob_terms, 'fsdp')  13.9 us
    dot_general x1, matrix products, local(): lax.dot_general(grad_rows, w_down, back_dims, preferred_element_type=jnp....  7.96 us
    dot_general x1, matrix products, local(): gate_proj = jnp.dot(expert_rows, w_gate, preferred_element_type=jnp.float32)  7.81 us
  transfers between devices with their start and end apart: 8, of which 6 were waited for; matrix products, arithmetic and copies ran while one was open for 16% of the time, Pallas kernels for 0%

commit v1 on v0

--- a/solution.py
+++ b/solution.py
@@ -44,7 +44,14 @@
         return jnp.repeat(placed, groups, axis=0)
 
     def to_expert_layout(source, scaled):
-        joined = lax.all_gather(source, "fsdp", axis=1, tiled=True)
+        ring = [source]
+        for hop in range(7):
+            ring.append(lax.ppermute(ring[-1], "fsdp", [(dev, (dev + 1) % 8) for dev in range(8)]))
+        joined = jnp.roll(
+            jnp.concatenate(ring[::-1], axis=1),
+            (lax.axis_index("fsdp") + 1) * ring[0].shape[1],
+            axis=1,
+        )
         arrived = lax.all_to_all(
             place_rows(joined, scaled), "dp", split_axis=0, concat_axis=0, tiled=True
         )

time: 348 us -> 331 us (0.951)
  starting transfers between devices: 47 us -> 32.5 us
    ppermute x0 -> x14, waiting for transfers between devices: none -> 75.7 us  [to_expert_layout(): lax.ppermute(ring[-1], 'fsdp', [(dev, (dev + 1) % 8) for dev in range(8)])]
    all_gather x2 -> x0, waiting for transfers between devices: 49.5 us -> none  [to_expert_layout(): joined = lax.all_gather(source, 'fsdp', axis=1, tiled=True)]
    all_to_all x2, waiting for transfers between devices: 91.5 us -> 64.4 us  [to_expert_layout(): lax.all_to_all(place_rows(joined, scaled), 'dp', split_axis=0, concat_axi...]
    all_to_all x2, starting transfers between devices: 31.5 us -> 17.1 us  [to_expert_layout(): lax.all_to_all(place_rows(joined, scaled), 'dp', split_axis=0, concat_axi...]
  transfers between devices with their start and end apart: 8 -> 20, of which waited for: 6 -> 18; matrix products, arithmetic and copies ran while one was open for 16% -> 16% of each run, Pallas kernels for 0% -> 0%
where the time goes in v1:
time: 331 us; the launch traced here: 330 us
  waiting for transfers between devices  194 us (59%)
  matrix products  65.2 us (20%)
  starting transfers between devices  32.5 us (10%)
  between operations  14.3 us (4%)
  blocking collectives  13.9 us (4%)
  local copies, waits for them, and re-layouts  8.55 us (3%)
    ppermute x14, waiting for transfers between devices, to_expert_layout(): lax.ppermute(ring[-1], 'fsdp', [(dev, (dev + 1) % 8) for dev in range(8)])  75.7 us
    all_to_all x2, waiting for transfers between devices, to_expert_layout(): lax.all_to_all(place_rows(joined, scaled), 'dp', split_axis=0, concat_axi...  64.4 us
    reduce_scatter x2, waiting for transfers between devices, to_token_layout(): lax.psum_scatter(partial_value.astype(jnp.bfloat16), 'fsdp', scatter_dime...  53.8 us
    all_to_all x2, starting transfers between devices, to_expert_layout(): lax.all_to_all(place_rows(joined, scaled), 'dp', split_axis=0, concat_axi...  17.1 us
    all_to_all x2, starting transfers between devices, to_token_layout(): lax.all_to_all(shares.reshape(dp_count, CAP, shares.shape[1]).astype(jnp....  14.9 us
    psum x1, blocking collectives, local(): prob_grad = lax.psum(prob_terms, 'fsdp')  13.9 us
    dot_general x1, matrix products, local(): lax.dot_general(grad_rows, w_down, back_dims, preferred_element_type=jnp....  7.96 us
    dot_general x1, matrix products, local(): gate_proj = jnp.dot(expert_rows, w_gate, preferred_element_type=jnp.float32)  7.81 us
  transfers between devices with their start and end apart: 20, of which 18 were waited for; matrix products, arithmetic and copies ran while one was open for 16% of the time, Pallas kernels for 0%

profile of v1, /device:TPU:2, one launch (start us, length us, event | category | flops | bytes accessed | tf_op | source)
XLA Modules:
  0.0 329.9 jit_solution(3168089815974672454)
XLA Ops:
  7.2 5.8 %collective-permute-done = bf16[128,512]{1,0:T(8,128)(2,1)S(1)} collective-permute-done((bf16[128,512]{1,0:T(8,128)(2,1)}, bf16[128,512]{1,0:T(8,128)(2,1)S(1)}, u32[]{:S(2)}, u32[]{:S(2)}) %collective-permute-start) | collective-permute-done | bytes 131104 | tf_op jit(solution)/shard_map/ppermute | solution.py:49
  13.0 5.6 %collective-permute-done.1 = bf16[128,512]{1,0:T(8,128)(2,1)S(1)} collective-permute-done((bf16[128,512]{1,0:T(8,128)(2,1)S(1)}, bf16[128,512]{1,0:T(8,128)(2,1)S(1)}, u32[]{:S(2)}, u32[]{:S(2)}) %collective-permute-start.1) | collective-permute-done | bytes 131104 | tf_op jit(solution)/shard_map/ppermute | solution.py:49
  41.0 5.6 %collective-permute-done.6 = bf16[128,512]{1,0:T(8,128)(2,1)S(1)} collective-permute-done((bf16[128,512]{1,0:T(8,128)(2,1)S(1)}, bf16[128,512]{1,0:T(8,128)(2,1)S(1)}, u32[]{:S(2)}, u32[]{:S(2)}) %collective-permute-start.6) | collective-permute-done | bytes 131104 | tf_op jit(solution)/shard_map/ppermute | solution.py:49
  51.6 8.5 %all-to-all-start = ((bf16[16,40,4096]{2,1,0:T(8,128)(2,1)}), bf16[16,40,4096]{2,1,0:T(8,128)(2,1)}, u32[]{:S(2)}, u32[]{:S(2)}) async-start(bf16[16,40,4096]{2,1,0:T(8,128)(2,1)} %bitcast.55), calls=%async_computation | async-start | bytes 10485760 | tf_op jit(solution)/shard_map/all_to_all | solution.py:55
  65.7 5.6 %collective-permute-done.8 = bf16[128,512]{1,0:T(8,128)(2,1)S(1)} collective-permute-done((bf16[128,512]{1,0:T(8,128)(2,1)S(1)}, bf16[128,512]{1,0:T(8,128)(2,1)S(1)}, u32[]{:S(2)}, u32[]{:S(2)}) %collective-permute-start.8) | collective-permute-done | bytes 131104 | tf_op jit(solution)/shard_map/ppermute | solution.py:49
  71.3 5.6 %collective-permute-done.9 = bf16[128,512]{1,0:T(8,128)(2,1)S(1)} collective-permute-done((bf16[128,512]{1,0:T(8,128)(2,1)S(1)}, bf16[128,512]{1,0:T(8,128)(2,1)S(1)}, u32[]{:S(2)}, u32[]{:S(2)}) %collective-permute-start.9) | collective-permute-done | bytes 131104 | tf_op jit(solution)/shard_map/ppermute | solution.py:49
  76.9 5.6 %collective-permute-done.10 = bf16[128,512]{1,0:T(8,128)(2,1)S(1)} collective-permute-done((bf16[128,512]{1,0:T(8,128)(2,1)S(1)}, bf16[128,512]{1,0:T(8,128)(2,1)S(1)}, u32[]{:S(2)}, u32[]{:S(2)}) %collective-permute-start.10) | collective-permute-done | bytes 131104 | tf_op jit(solution)/shard_map/ppermute | solution.py:49
  82.5 5.6 %collective-permute-done.11 = bf16[128,512]{1,0:T(8,128)(2,1)S(1)} collective-permute-done((bf16[128,512]{1,0:T(8,128)(2,1)S(1)}, bf16[128,512]{1,0:T(8,128)(2,1)S(1)}, u32[]{:S(2)}, u32[]{:S(2)}) %collective-permute-start.11) | collective-permute-done | bytes 131104 | tf_op jit(solution)/shard_map/ppermute | solution.py:49
  88.1 5.6 %collective-permute-done.12 = bf16[128,512]{1,0:T(8,128)(2,1)S(1)} collective-permute-done((bf16[128,512]{1,0:T(8,128)(2,1)S(1)}, bf16[128,512]{1,0:T(8,128)(2,1)S(1)}, u32[]{:S(2)}, u32[]{:S(2)}) %collective-permute-start.12) | collective-permute-done | bytes 131104 | tf_op jit(solution)/shard_map/ppermute | solution.py:49
  93.7 5.6 %collective-permute-done.13 = bf16[128,512]{1,0:T(8,128)(2,1)S(1)} collective-permute-done((bf16[128,512]{1,0:T(8,128)(2,1)S(1)}, bf16[128,512]{1,0:T(8,128)(2,1)S(1)}, u32[]{:S(2)}, u32[]{:S(2)}) %collective-permute-start.13) | collective-permute-done | bytes 131104 | tf_op jit(solution)/shard_map/ppermute | solution.py:49
  101.8 18.1 %all-to-all-done = bf16[16,40,4096]{2,1,0:T(8,128)(2,1)} async-done(((bf16[16,40,4096]{2,1,0:T(8,128)(2,1)}), bf16[16,40,4096]{2,1,0:T(8,128)(2,1)}, u32[]{:S(2)}, u32[]{:S(2)}) %all-to-all-start) | async-done | bytes 5242912 | tf_op jit(solution)/shard_map/all_to_all | solution.py:55
  123.0 8.6 %all-to-all-start.2 = ((bf16[16,40,4096]{2,1,0:T(8,128)(2,1)}), bf16[16,40,4096]{2,1,0:T(8,128)(2,1)}, u32[]{:S(2)}, u32[]{:S(2)}) async-start(bf16[16,40,4096]{2,1,0:T(8,128)(2,1)} %bitcast.56), calls=%async_computation.3 | async-start | bytes 10485760 | tf_op jit(solution)/shard_map/all_to_all | solution.py:55
  131.8 7.8 %fusion.34 = f32[640,512]{1,0:T(8,128)} fusion(bf16[640,4096]{1,0:T(8,128)(2,1)} %bitcast.7, bf16[4096,512]{1,0:T(8,128)(2,1)} %param.12), kind=kOutput, calls=%fused_computation.79 | convolution fusion | flops 2684354560 | bytes 10747904 | tf_op jit(solution)/shard_map/dot_general | solution.py:76
  139.6 6.4 %fusion.35 = f32[640,512]{1,0:T(8,128)} fusion(bf16[640,4096]{1,0:T(8,128)(2,1)} %bitcast.7, bf16[4096,512]{1,0:T(8,128)(2,1)S(1)} %copy-done.3), kind=kOutput, calls=%fused_computation.80 | convolution fusion | flops 2684354560 | bytes 10747904 | tf_op jit(solution)/shard_map/dot_general | solution.py:77
  146.1 46.3 %all-to-all-done.2 = bf16[16,40,4096]{2,1,0:T(8,128)(2,1)} async-done(((bf16[16,40,4096]{2,1,0:T(8,128)(2,1)}), bf16[16,40,4096]{2,1,0:T(8,128)(2,1)}, u32[]{:S(2)}, u32[]{:S(2)}) %all-to-all-start.2) | async-done | bytes 5242912 | tf_op jit(solution)/shard_map/all_to_all | solution.py:55
  192.3 8.0 %multiply_convert_fusion = (bf16[640,512]{1,0:T(8,128)(2,1)S(1)}, bf16[640,512]{1,0:T(8,128)(2,1)S(1)}, bf16[640,512]{1,0:T(8,128)(2,1)S(1)}) fusion(f32[640,512]{1,0:T(8,128)} %fusion.34, f32[640,512]{1,0:T(8,128)} %fusion.35, bf16[640,4096]{1,0:T(8,128)(2,1)} %bitcast.14, bf16[512,4096]{1,0:T(8,128)(2,1)} %param.14), kind=kOutput, calls=%fused_computation.13 | convolution fusion | flops 2689269760 | bytes 14024704 | tf_op jit(solution)/shard_map/dot_general | solution.py:105
  215.0 7.5 %convolution_convert_fusion.1 = bf16[512,4096]{1,0:T(8,128)(2,1)} fusion(bf16[640,512]{1,0:T(8,128)(2,1)S(1)} %get-tuple-element.11, bf16[640,4096]{1,0:T(8,128)(2,1)} %bitcast.14), kind=kOutput, calls=%fused_computation.2 | convolution fusion | flops 2686451712 | bytes 10092544 | tf_op jit(solution)/shard_map/dot_general | solution.py:116
  222.5 7.5 %convolution_convert_fusion.2 = bf16[4096,512]{1,0:T(8,128)(2,1)} fusion(bf16[640,4096]{1,0:T(8,128)(2,1)} %bitcast.7, bf16[640,512]{1,0:T(8,128)(2,1)S(1)} %get-tuple-element.9), kind=kOutput, calls=%fused_computation.3 | convolution fusion | flops 2686451712 | bytes 10092544 | tf_op jit(solution)/shard_map/dot_general | solution.py:113
  230.0 27.0 %reduce-scatter.3.cloned.1.call-done = bf16[640,512]{1,0:T(8,128)(2,1)} async-done(((bf16[640,4096]{1,0:T(8,128)(2,1)}), bf16[640,512]{1,0:T(8,128)(2,1)}) %reduce-scatter.3.cloned.1.call-update) | async-done | bytes 655376 | tf_op jit(solution)/shard_map/reduce_scatter | solution.py:61
  257.0 7.4 %all-to-all-start.1 = ((bf16[16,40,512]{2,1,0:T(8,128)(2,1)}), bf16[16,40,512]{2,1,0:T(8,128)(2,1)S(1)}, u32[]{:S(2)}, u32[]{:S(2)}) async-start(bf16[16,40,512]{2,1,0:T(8,128)(2,1)} %bitcast.63), calls=%async_computation.2 | async-start | bytes 1310720 | tf_op jit(solution)/shard_map/all_to_all | solution.py:64
  264.5 7.6 %convolution_convert_fusion.3 = bf16[4096,512]{1,0:T(8,128)(2,1)} fusion(bf16[640,4096]{1,0:T(8,128)(2,1)} %bitcast.7, bf16[640,512]{1,0:T(8,128)(2,1)S(1)} %get-tuple-element.10), kind=kOutput, calls=%fused_computation.4 | convolution fusion | flops 2686451712 | bytes 10092544 | tf_op jit(solution)/shard_map/dot_general | solution.py:110
  272.0 26.8 %reduce-scatter.5.cloned.1.call-done = bf16[640,512]{1,0:T(8,128)(2,1)} async-done(((bf16[640,4096]{1,0:T(8,128)(2,1)}), bf16[640,512]{1,0:T(8,128)(2,1)}) %reduce-scatter.5.cloned.1.call-update) | async-done | bytes 655376 | tf_op jit(solution)/shard_map/reduce_scatter | solution.py:61
  298.9 7.4 %all-to-all-start.3 = ((bf16[16,40,512]{2,1,0:T(8,128)(2,1)}), bf16[16,40,512]{2,1,0:T(8,128)(2,1)S(1)}, u32[]{:S(2)}, u32[]{:S(2)}) async-start(bf16[16,40,512]{2,1,0:T(8,128)(2,1)} %bitcast.62), calls=%async_computation.5 | async-start | bytes 1310720 | tf_op jit(solution)/shard_map/all_to_all | solution.py:64
  308.0 13.9 %psum.7 = f32[128,2]{0,1:T(2,128)} all-reduce(f32[128,2]{0,1:T(2,128)S(1)} %pad_maximum_fusion), channel_id=1, replica_groups=mesh['dp'=16,'fsdp'=8] {'fsdp'}, use_global_device_ids=true, to_apply=%region_9.11 | all-reduce | flops 256 | bytes 2048 | tf_op jit(solution)/shard_map/psum | solution.py:103
  (78 shorter events, 56.2 us)
Async XLA Ops:
  7.2 5.8 %collective-permute-start = (bf16[128,512]{1,0:T(8,128)(2,1)}, bf16[128,512]{1,0:T(8,128)(2,1)S(1)}, u32[]{:S(2)}, u32[]{:S(2)}) collective-permute-start(bf16[128,512]{1,0:T(8,128)(2,1)} %param.9), channel_id=1, source_target_pairs={{0,1},{1,2},{2,3},{3,4},{4,5},{5,6},{6,7},{7,0},{8,9},{9,10},{10,1... | collective-permute-start | bytes 393224 | tf_op jit(solution)/shard_map/ppermute | solution.py:49
  13.0 5.6 %collective-permute-start.1 = (bf16[128,512]{1,0:T(8,128)(2,1)S(1)}, bf16[128,512]{1,0:T(8,128)(2,1)S(1)}, u32[]{:S(2)}, u32[]{:S(2)}) collective-permute-start(bf16[128,512]{1,0:T(8,128)(2,1)S(1)} %collective-permute-done), channel_id=1, source_target_pairs={{0,1},{1,2},{2,3},{3,4},{4,5},{5,6},{6,7},{7,0},{8,9},{9,10},{10,1... | collective-permute-start | bytes 393224 | tf_op jit(solution)/shard_map/ppermute | solution.py:49
  18.6 5.6 %collective-permute-start.2 = (bf16[128,512]{1,0:T(8,128)(2,1)S(1)}, bf16[128,512]{1,0:T(8,128)(2,1)S(1)}, u32[]{:S(2)}, u32[]{:S(2)}) collective-permute-start(bf16[128,512]{1,0:T(8,128)(2,1)S(1)} %collective-permute-done.1), channel_id=1, source_target_pairs={{0,1},{1,2},{2,3},{3,4},{4,5},{5,6},{6,7},{7,0},{8,9},{9,10},{10,1... | collective-permute-start | bytes 393224 | tf_op jit(solution)/shard_map/ppermute | solution.py:49
  24.2 5.6 %collective-permute-start.3 = (bf16[128,512]{1,0:T(8,128)(2,1)S(1)}, bf16[128,512]{1,0:T(8,128)(2,1)S(1)}, u32[]{:S(2)}, u32[]{:S(2)}) collective-permute-start(bf16[128,512]{1,0:T(8,128)(2,1)S(1)} %collective-permute-done.2), channel_id=1, source_target_pairs={{0,1},{1,2},{2,3},{3,4},{4,5},{5,6},{6,7},{7,0},{8,9},{9,10},{10,1... | collective-permute-start | bytes 393224 | tf_op jit(solution)/shard_map/ppermute | solution.py:49
  29.8 5.6 %collective-permute-start.4 = (bf16[128,512]{1,0:T(8,128)(2,1)S(1)}, bf16[128,512]{1,0:T(8,128)(2,1)S(1)}, u32[]{:S(2)}, u32[]{:S(2)}) collective-permute-start(bf16[128,512]{1,0:T(8,128)(2,1)S(1)} %collective-permute-done.3), channel_id=1, source_target_pairs={{0,1},{1,2},{2,3},{3,4},{4,5},{5,6},{6,7},{7,0},{8,9},{9,10},{10,1... | collective-permute-start | bytes 393224 | tf_op jit(solution)/shard_map/ppermute | solution.py:49
  35.4 5.6 %collective-permute-start.5 = (bf16[128,512]{1,0:T(8,128)(2,1)S(1)}, bf16[128,512]{1,0:T(8,128)(2,1)S(1)}, u32[]{:S(2)}, u32[]{:S(2)}) collective-permute-start(bf16[128,512]{1,0:T(8,128)(2,1)S(1)} %collective-permute-done.4), channel_id=1, source_target_pairs={{0,1},{1,2},{2,3},{3,4},{4,5},{5,6},{6,7},{7,0},{8,9},{9,10},{10,1... | collective-permute-start | bytes 393224 | tf_op jit(solution)/shard_map/ppermute | solution.py:49
  41.0 5.6 %collective-permute-start.6 = (bf16[128,512]{1,0:T(8,128)(2,1)S(1)}, bf16[128,512]{1,0:T(8,128)(2,1)S(1)}, u32[]{:S(2)}, u32[]{:S(2)}) collective-permute-start(bf16[128,512]{1,0:T(8,128)(2,1)S(1)} %collective-permute-done.5), channel_id=1, source_target_pairs={{0,1},{1,2},{2,3},{3,4},{4,5},{5,6},{6,7},{7,0},{8,9},{9,10},{10,1... | collective-permute-start | bytes 393224 | tf_op jit(solution)/shard_map/ppermute | solution.py:49
  51.6 8.5 %copy-start = (bf16[128,512]{1,0:T(8,128)(2,1)S(1)}, bf16[128,512]{1,0:T(8,128)(2,1)}, u32[]{:S(2)}) copy-start(bf16[128,512]{1,0:T(8,128)(2,1)} %param.15) | copy-start | bytes 393220
  51.6 42.1 %copy-start.1 = (f32[128,2]{0,1:T(2,128)S(1)}, f32[128,2]{0,1:T(2,128)}, u32[]{:S(2)}) copy-start(f32[128,2]{0,1:T(2,128)} %param.11) | copy-start | bytes 3076
  51.6 68.4 %all-to-all-start = ((bf16[16,40,4096]{2,1,0:T(8,128)(2,1)}), bf16[16,40,4096]{2,1,0:T(8,128)(2,1)}, u32[]{:S(2)}, u32[]{:S(2)}) async-start(bf16[16,40,4096]{2,1,0:T(8,128)(2,1)} %bitcast.55), calls=%async_computation | async-start | bytes 10485760 | tf_op jit(solution)/shard_map/all_to_all | solution.py:55
  60.1 5.6 %collective-permute-start.7 = (bf16[128,512]{1,0:T(8,128)(2,1)S(1)}, bf16[128,512]{1,0:T(8,128)(2,1)S(1)}, u32[]{:S(2)}, u32[]{:S(2)}) collective-permute-start(bf16[128,512]{1,0:T(8,128)(2,1)S(1)} %copy-done), channel_id=1, source_target_pairs={{0,1},{1,2},{2,3},{3,4},{4,5},{5,6},{6,7},{7,0},{8,9},{9,10},{10,1... | collective-permute-start | bytes 393224 | tf_op jit(solution)/shard_map/ppermute | solution.py:49
  65.7 5.6 %collective-permute-start.8 = (bf16[128,512]{1,0:T(8,128)(2,1)S(1)}, bf16[128,512]{1,0:T(8,128)(2,1)S(1)}, u32[]{:S(2)}, u32[]{:S(2)}) collective-permute-start(bf16[128,512]{1,0:T(8,128)(2,1)S(1)} %collective-permute-done.7), channel_id=1, source_target_pairs={{0,1},{1,2},{2,3},{3,4},{4,5},{5,6},{6,7},{7,0},{8,9},{9,10},{10,1... | collective-permute-start | bytes 393224 | tf_op jit(solution)/shard_map/ppermute | solution.py:49
  71.3 5.6 %collective-permute-start.9 = (bf16[128,512]{1,0:T(8,128)(2,1)S(1)}, bf16[128,512]{1,0:T(8,128)(2,1)S(1)}, u32[]{:S(2)}, u32[]{:S(2)}) collective-permute-start(bf16[128,512]{1,0:T(8,128)(2,1)S(1)} %collective-permute-done.8), channel_id=1, source_target_pairs={{0,1},{1,2},{2,3},{3,4},{4,5},{5,6},{6,7},{7,0},{8,9},{9,10},{10,1... | collective-permute-start | bytes 393224 | tf_op jit(solution)/shard_map/ppermute | solution.py:49
  76.9 5.6 %collective-permute-start.10 = (bf16[128,512]{1,0:T(8,128)(2,1)S(1)}, bf16[128,512]{1,0:T(8,128)(2,1)S(1)}, u32[]{:S(2)}, u32[]{:S(2)}) collective-permute-start(bf16[128,512]{1,0:T(8,128)(2,1)S(1)} %collective-permute-done.9), channel_id=1, source_target_pairs={{0,1},{1,2},{2,3},{3,4},{4,5},{5,6},{6,7},{7,0},{8,9},{9,10},{10,1... | collective-permute-start | bytes 393224 | tf_op jit(solution)/shard_map/ppermute | solution.py:49
  82.5 5.6 %collective-permute-start.11 = (bf16[128,512]{1,0:T(8,128)(2,1)S(1)}, bf16[128,512]{1,0:T(8,128)(2,1)S(1)}, u32[]{:S(2)}, u32[]{:S(2)}) collective-permute-start(bf16[128,512]{1,0:T(8,128)(2,1)S(1)} %collective-permute-done.10), channel_id=1, source_target_pairs={{0,1},{1,2},{2,3},{3,4},{4,5},{5,6},{6,7},{7,0},{8,9},{9,10},{10,1... | collective-permute-start | bytes 393224 | tf_op jit(solution)/shard_map/ppermute | solution.py:49
  88.1 5.6 %collective-permute-start.12 = (bf16[128,512]{1,0:T(8,128)(2,1)S(1)}, bf16[128,512]{1,0:T(8,128)(2,1)S(1)}, u32[]{:S(2)}, u32[]{:S(2)}) collective-permute-start(bf16[128,512]{1,0:T(8,128)(2,1)S(1)} %collective-permute-done.11), channel_id=1, source_target_pairs={{0,1},{1,2},{2,3},{3,4},{4,5},{5,6},{6,7},{7,0},{8,9},{9,10},{10,1... | collective-permute-start | bytes 393224 | tf_op jit(solution)/shard_map/ppermute | solution.py:49
  93.7 5.6 %collective-permute-start.13 = (bf16[128,512]{1,0:T(8,128)(2,1)S(1)}, bf16[128,512]{1,0:T(8,128)(2,1)S(1)}, u32[]{:S(2)}, u32[]{:S(2)}) collective-permute-start(bf16[128,512]{1,0:T(8,128)(2,1)S(1)} %collective-permute-done.12), channel_id=1, source_target_pairs={{0,1},{1,2},{2,3},{3,4},{4,5},{5,6},{6,7},{7,0},{8,9},{9,10},{10,1... | collective-permute-start | bytes 393224 | tf_op jit(solution)/shard_map/ppermute | solution.py:49
  123.0 69.4 %all-to-all-start.2 = ((bf16[16,40,4096]{2,1,0:T(8,128)(2,1)}), bf16[16,40,4096]{2,1,0:T(8,128)(2,1)}, u32[]{:S(2)}, u32[]{:S(2)}) async-start(bf16[16,40,4096]{2,1,0:T(8,128)(2,1)} %bitcast.56), calls=%async_computation.3 | async-start | bytes 10485760 | tf_op jit(solution)/shard_map/all_to_all | solution.py:55
  131.6 125.5 %reduce-scatter.3.cloned.1.call-start = ((), (), s32[]{:S(2)}) async-start(), calls=%async_computation.6 | async-start | bytes 5898240 | tf_op jit(solution)/shard_map/reduce_scatter | solution.py:61
  131.8 7.8 %copy-start.3 = (bf16[4096,512]{1,0:T(8,128)(2,1)S(1)}, bf16[4096,512]{1,0:T(8,128)(2,1)}, u32[]{:S(2)}) copy-start(bf16[4096,512]{1,0:T(8,128)(2,1)} %param.13) | copy-start | bytes 12582916
  192.3 8.0 %copy-start.2 = (bf16[512,4096]{1,0:T(8,128)(2,1)S(1)}, bf16[512,4096]{1,0:T(8,128)(2,1)}, u32[]{:S(2)}) copy-start(bf16[512,4096]{1,0:T(8,128)(2,1)} %param.14) | copy-start | bytes 12582916
  205.0 93.8 %reduce-scatter.5.cloned.1.call-start = ((), (), s32[]{:S(2)}) async-start(), calls=%async_computation.7 | async-start | bytes 5898240 | tf_op jit(solution)/shard_map/reduce_scatter | solution.py:61
  257.0 41.8 %all-to-all-start.1 = ((bf16[16,40,512]{2,1,0:T(8,128)(2,1)}), bf16[16,40,512]{2,1,0:T(8,128)(2,1)S(1)}, u32[]{:S(2)}, u32[]{:S(2)}) async-start(bf16[16,40,512]{2,1,0:T(8,128)(2,1)} %bitcast.63), calls=%async_computation.2 | async-start | bytes 1310720 | tf_op jit(solution)/shard_map/all_to_all | solution.py:64
  298.9 23.0 %all-to-all-start.3 = ((bf16[16,40,512]{2,1,0:T(8,128)(2,1)}), bf16[16,40,512]{2,1,0:T(8,128)(2,1)S(1)}, u32[]{:S(2)}, u32[]{:S(2)}) async-start(bf16[16,40,512]{2,1,0:T(8,128)(2,1)} %bitcast.62), calls=%async_computation.5 | async-start | bytes 1310720 | tf_op jit(solution)/shard_map/all_to_all | solution.py:64
  (1 other events, 4.9 us)
Sparse Core Ops, SparseCore 0:
  205.2 51.8 reduce-scatter.2
  259.4 39.3 reduce-scatter.4
